TPU v7x, 32 devices: a whole 2x2x4 slice. The times are simulated.
32 devices in a mesh: section: 2 (over core), dp: 16 (over z, y, x).
Axes of the slice: x: 2, y: 2, z: 4, core: 2. Of those that a mesh axis runs over, the one named last changes fastest.
Arguments:
- acts: bfloat16 [2, 16, 1, 64, 2, 2, 128], P('section', 'dp'), may hold values from -6 to 6
- preacts: bfloat16 [2, 16, 1, 64, 2, 2, 128], P('section', 'dp'), may hold values from -6 to 6
- top_grad: bfloat16 [16, 1, 64, 2, 2, 128], P('dp'), may hold values from -6 to 6
- weights: bfloat16 [2, 64, 1728], P('section'), may hold values from -0.21875 to 0.21875
- a_factor: bfloat16 [2, 1728, 1728], P('section', 'dp'), as said below
- g_factor: bfloat16 [2, 64, 64], P('section'), as said below
Outputs:
- act_grads: bfloat16 [2, 16, 1, 64, 2, 2, 128], P('section', 'dp')
- update: float32 [2, 1728, 64], P('section', 'dp')
- inverse: float32 [2, 1728, 1728], P('section', 'dp')
Inputs may be any that keep to these rules, and one draw needn't show every extreme that they name: `a_factor`: each matrix is symmetric and positive definite. `g_factor`: each matrix is symmetric and positive definite.
All inputs are finite; a program needn't handle non-finite values. Where the computation divides by a largest or mean magnitude, that divisor is 1e-20 or more.
Results may differ from a plain program's by a relative error of at most 0.006.
Values may be sent and summed in bfloat16 or wider, within the bound.
No kernel may reach another device: no remote copies, remote signals or barrier semaphores. Data moves between devices by JAX's collectives and lax.ppermute only.
A program may use at most 64 MiB of HBM per device.

v0:
```python
import jax
import jax.numpy as jnp
from jax import lax
from jax.sharding import PartitionSpec as P

KW = 3
MICRO = 1


def shifted(value, axis, steps):
    count = lax.axis_size(axis)
    first, last = (max(0, -steps), min(count, count - steps))
    return lax.ppermute(value, axis, [(source, source + steps) for source in range(first, last)])


def tap_offsets(kernel_width):
    middle = kernel_width // 2
    result = []
    for along_x in range(kernel_width):
        for along_y in range(kernel_width):
            for along_z in range(kernel_width):
                result.append((along_x - middle, along_y - middle, along_z - middle))
    return result


def taps_stack(volume, kernel_width, direction):
    middle = kernel_width // 2
    padded = jnp.pad(volume, ((0, 0), (middle, middle), (middle, middle), (middle, middle)))
    size_x, size_y, size_z = (volume.shape[1], volume.shape[2], volume.shape[3])
    pieces = []
    for off_x, off_y, off_z in tap_offsets(kernel_width):
        start_x = middle + direction * off_x
        start_y = middle + direction * off_y
        start_z = middle + direction * off_z
        pieces.append(
            padded[
                :,
                start_x : start_x + size_x,
                start_y : start_y + size_y,
                start_z : start_z + size_z,
            ]
        )
    stacked = jnp.stack(pieces, 0)
    return stacked.reshape(len(pieces) * volume.shape[0], size_x * size_y * size_z)


def back_input(grad_out, w_rows):
    columns = taps_stack(grad_out, KW, -1)
    summed = lax.dot_general(
        w_rows, columns, (((0,), (0,)), ((), ())), preferred_element_type=jnp.float32
    )
    return summed.astype(jnp.bfloat16).reshape(grad_out.shape)


def back_weight(volume, grad_out):
    columns = taps_stack(volume, KW, 1)
    flattened = grad_out.reshape(grad_out.shape[0], -1)
    return lax.dot_general(
        columns, flattened, (((1,), (1,)), ((), ())), preferred_element_type=jnp.float32
    )


def local_inverse(matrix):
    values = matrix.astype(jnp.float32)
    step_size = 1.0 / jnp.max(jnp.sum(jnp.abs(values), axis=1))
    identity = jnp.eye(matrix.shape[0], dtype=jnp.float32)
    resid0 = (identity - step_size * values).astype(jnp.bfloat16)
    resid1 = jnp.dot(resid0, resid0, preferred_element_type=jnp.float32).astype(jnp.bfloat16)
    cross_term = jnp.dot(resid1, resid0, preferred_element_type=jnp.float32)
    return step_size * (
        identity + resid0.astype(jnp.float32) + resid1.astype(jnp.float32) + cross_term
    )


def eye_rows(start_row, row_total, order_full):
    column_ids = lax.broadcasted_iota(jnp.int32, (row_total, order_full), 1)
    row_ids = lax.broadcasted_iota(jnp.int32, (row_total, order_full), 0)
    return (column_ids == start_row + row_ids).astype(jnp.float32)


def shards(acts, preacts, top_grad, weights, a_factor, g_factor):
    section_index = lax.axis_index("section")
    section_count = lax.axis_size("section")
    tick_count = MICRO + section_count - 1
    inputs = acts[0, 0]
    pre_values = preacts[0, 0]
    upper_grads = top_grad[0]
    channels = weights.shape[1]
    w_rows = weights[0].reshape(channels, -1, channels).transpose(1, 0, 2).reshape(-1, channels)
    zero_field = jnp.zeros(inputs.shape[1:], jnp.bfloat16)

    def one_tick(tick_index, carried):
        outgoing, stored_grads, stored_slopes = carried
        incoming = shifted(outgoing, "section", -1)
        micro_index = tick_index - (section_count - 1 - section_index)
        is_valid = jnp.logical_and(micro_index >= 0, micro_index < MICRO)
        clipped = jnp.clip(micro_index, 0, MICRO - 1)
        from_top = lax.dynamic_index_in_dim(upper_grads, clipped, 0, keepdims=False)
        arriving = jnp.where(section_index == section_count - 1, from_top, incoming)
        pre_now = lax.dynamic_index_in_dim(pre_values, clipped, 0, keepdims=False)
        grad_out = jnp.where(pre_now > 0, arriving, zero_field)
        sending = back_input(grad_out, w_rows)
        old_grad = lax.dynamic_index_in_dim(stored_grads, clipped, 0, keepdims=False)
        old_slope = lax.dynamic_index_in_dim(stored_slopes, clipped, 0, keepdims=False)
        stored_grads = lax.dynamic_update_index_in_dim(
            stored_grads, jnp.where(is_valid, sending, old_grad), clipped, 0
        )
        stored_slopes = lax.dynamic_update_index_in_dim(
            stored_slopes, jnp.where(is_valid, grad_out, old_slope), clipped, 0
        )
        return (sending, stored_grads, stored_slopes)

    start_state = (
        zero_field,
        jnp.zeros(inputs.shape, jnp.bfloat16),
        jnp.zeros(inputs.shape, jnp.bfloat16),
    )
    last_sent, stored_grads, stored_slopes = lax.fori_loop(0, tick_count, one_tick, start_state)
    local_grad = back_weight(inputs[0], stored_slopes[0])
    summed_grad = lax.psum(local_grad, "dp")
    mean_grad = summed_grad / lax.axis_size("dp")
    a_rows = a_factor[0]
    row_total = a_rows.shape[0]
    order_full = a_rows.shape[1]
    first_row = lax.axis_index("dp") * row_total
    local_max = jnp.max(jnp.sum(jnp.abs(a_rows.astype(jnp.float32)), axis=1))
    step_size = 1.0 / lax.pmax(local_max, "dp")
    own_eye = eye_rows(first_row, row_total, order_full)
    resid0 = (own_eye - step_size * a_rows.astype(jnp.float32)).astype(jnp.bfloat16)
    left_cols = resid0
    resid1 = jnp.dot(
        left_cols,
        lax.all_gather(resid0, "dp", axis=0, tiled=True),
        preferred_element_type=jnp.float32,
    ).astype(jnp.bfloat16)
    left_cols = resid1
    cross_term = jnp.dot(
        left_cols,
        lax.all_gather(resid0, "dp", axis=0, tiled=True),
        preferred_element_type=jnp.float32,
    )
    inverse_rows = step_size * (
        own_eye + resid0.astype(jnp.float32) + resid1.astype(jnp.float32) + cross_term
    )
    g_inverse = local_inverse(g_factor[0])
    preconditioned = jnp.dot(
        mean_grad, g_inverse, precision=lax.Precision.HIGHEST, preferred_element_type=jnp.float32
    )
    update_rows = jnp.dot(
        inverse_rows,
        preconditioned,
        precision=lax.Precision.HIGHEST,
        preferred_element_type=jnp.float32,
    )
    return (stored_grads[None, None], update_rows[None], inverse_rows[None])


def solution(mesh):
    placed = (
        P("section", "dp", None, None, None, None, None),
        P("section", "dp", None, None, None, None, None),
        P("dp", None, None, None, None, None),
        P("section", None, None),
        P("section", "dp", None),
        P("section", None, None),
    )
    return jax.shard_map(
        shards,
        mesh=mesh,
        in_specs=placed,
        out_specs=(
            P("section", "dp", None, None, None, None, None),
            P("section", "dp", None),
            P("section", "dp", None),
        ),
        check_vma=False,
    )
```

profile of v0, /device:TPU:0, one launch (start us, length us, event | category | flops | bytes accessed | tf_op | source)
XLA Modules:
  0.0 278.0 jit_solution(16409648565365553291)
XLA Ops:
  7.2 1.5 reshape_squeeze.6
  8.7 0.9 copy.18
  13.2 2.1 reshape.70
  16.6 24.1 %while.20 = (s32[]{:T(128)}, bf16[64,2,2,128]{3,2,1,0:T(2,128)(2,1)}, bf16[1,64,2,2,128]{4,3,2,1,0:T(2,128)(2,1)}, bf16[1,64,2,2,128]{4,3,2,1,0:T(2,128)(2,1)}, ...) while((s32[]{:T(128)}, ...), condition=%wide.region_1.2_spmd.clone, body=%wide.region_0.1_spmd.clone.sunk | while | flops 113475592 | bytes 10772739 | solution.py:118
  16.6 1.3 collective-permute-start
  17.9 2.0 collective-permute-done
  20.0 1.7 fusion.173
  25.7 1.5 fusion.200
  28.6 1.3 collective-permute-start
  29.9 2.0 collective-permute-done
  32.0 1.7 fusion.173
  37.8 1.5 fusion.200
  40.7 0.9 reshape_squeeze.7
  42.2 2.9 %fusion.129 = f32[1728,64]{0,1:T(8,128)} fusion(bf16[1728,512]{1,0:T(8,128)(2,1)} %reshape.70, bf16[64,512]{1,0:T(8,128)(2,1)S(1)} %reshape_squeeze.7), kind=kOutput, calls=%fused_computation.203 | convolution fusion | flops 113246208 | bytes 2277376 | tf_op jit(solution)/shard_map/dot_general | solution.py:58
  45.2 44.4 %pmax.7 = f32[]{:T(128)} all-reduce(f32[]{:T(128)} %reduce_max.18), channel_id=1, replica_groups=mesh['section'=2,'dp'=16] {'dp'}, use_global_device_ids=true, to_apply=%region_4.5 | all-reduce | flops 1 | bytes 8 | tf_op jit(solution)/shard_map/pmax | solution.py:127
  90.3 1.0 fusion.128
  93.0 64.2 %all-reduce.4.cloned.1.call-done = f32[1728,64]{0,1:T(8,128)} async-done(((f32[1728,64]{0,1:T(8,128)}), f32[1728,64]{0,1:T(8,128)}) %all-reduce.4.cloned.1.call-update) | async-done | bytes 442384 | tf_op jit(solution)/shard_map/psum | solution.py:120
  157.1 1.6 fusion.60
  158.7 94.8 %all-gather.3.cloned.1.call-done = bf16[16,108,1728]{2,1,0:T(8,128)(2,1)} async-done(((bf16[1,108,1728]{2,1,0:T(8,128)(2,1)}), bf16[16,108,1728]{2,1,0:T(8,128)(2,1)}) %all-gather.3.cloned.1.call-update) | async-done | bytes 5971984 | tf_op jit(solution)/shard_map/all_gather | solution.py:133
  253.5 8.7 %reshape.72 = bf16[1728,1728]{1,0:T(8,128)(2,1)} reshape(bf16[16,108,1728]{2,1,0:T(8,128)(2,1)} %all-gather.3.cloned.1.call-done) | data formatting | bytes 11943936
  262.3 4.0 %convolution_convert_fusion.1 = bf16[108,1728]{1,0:T(8,128)(2,1)S(1)} fusion(bf16[1728,1728]{1,0:T(8,128)(2,1)} %reshape.72, bf16[1,108,1728]{2,1,0:T(8,128)(2,1)S(1)} %copy-done.3, f32[]{:T(128)S(6)} %div.12, s32[108]{0:T(128)S(1)} %iota_add_fusion), kind=kOutput, calls=%fused_computation.115 | convolution fusion | flops 646278912 | bytes 6718900 | tf_op jit(solution)/shard_map/dot_general | solution.py:131
  266.8 1.1 fusion.54
  267.9 1.6 convolution_bitcast_fusion
  269.5 1.7 copy.17
  (121 shorter events, 18.0 us)
Async XLA Ops:
  7.2 2.5 copy-start.2
  7.2 2.6 copy-start.1
  7.2 149.9 %all-reduce.4.cloned.1.call-start = ((), (), s32[]{:S(2)}) async-start(), calls=%async_computation | async-start | bytes 917504 | tf_op jit(solution)/shard_map/psum | solution.py:120
  16.6 3.3 %collective-permute-start = (bf16[64,2,2,128]{3,2,1,0:T(2,128)(2,1)}, bf16[64,2,2,128]{3,2,1,0:T(2,128)(2,1)S(1)}, u32[]{:S(2)}, u32[]{:S(2)}) collective-permute-start(bf16[64,2,2,128]{3,2,1,0:T(2,128)(2,1)} %get-tuple-element.362), channel_id=1, source_target_pairs={{16,0},{17,1},{18,2},{19,3},{20,4},{21,5},{22,6},{23,7},{24,8},{25... | collective-permute-start | bytes 196616 | tf_op jit(solution)/shard_map/while/body/eval_jaxpr/ppermute | solution.py:13
  25.7 2.2 copy-start.4
  28.0 0.6 copy-start.5
  28.6 3.3 %collective-permute-start = (bf16[64,2,2,128]{3,2,1,0:T(2,128)(2,1)}, bf16[64,2,2,128]{3,2,1,0:T(2,128)(2,1)S(1)}, u32[]{:S(2)}, u32[]{:S(2)}) collective-permute-start(bf16[64,2,2,128]{3,2,1,0:T(2,128)(2,1)} %get-tuple-element.362), channel_id=1, source_target_pairs={{16,0},{17,1},{18,2},{19,3},{20,4},{21,5},{22,6},{23,7},{24,8},{25... | collective-permute-start | bytes 196616 | tf_op jit(solution)/shard_map/while/body/eval_jaxpr/ppermute | solution.py:13
  37.8 2.2 copy-start.4
  40.1 0.6 copy-start.5
  40.7 49.6 %copy-start.3 = (bf16[1,108,1728]{2,1,0:T(8,128)(2,1)S(1)}, bf16[1,108,1728]{2,1,0:T(8,128)(2,1)}, u32[]{:S(2)}) copy-start(bf16[1,108,1728]{2,1,0:T(8,128)(2,1)} %param.12) | copy-start | bytes 1119748
  42.2 49.1 %copy-start.6 = (bf16[1,64,64]{2,1,0:T(8,128)(2,1)S(1)}, bf16[1,64,64]{2,1,0:T(8,128)(2,1)}, u32[]{:S(2)}) copy-start(bf16[1,64,64]{2,1,0:T(8,128)(2,1)} %param.13) | copy-start | bytes 24580
  45.1 208.4 %all-gather.3.cloned.1.call-start = ((), (), s32[]{:S(2)}) async-start(), calls=%async_computation.1 | async-start | bytes 6823936 | tf_op jit(solution)/shard_map/all_gather | solution.py:133
  262.3 4.5 %copy-start = (bf16[1728,1728]{1,0:T(8,128)(2,1)S(1)}, bf16[1728,1728]{1,0:T(8,128)(2,1)}, u32[]{:S(2)}) copy-start(bf16[1728,1728]{1,0:T(8,128)(2,1)} %reshape.72) | copy-start | bytes 17915908
Sparse Core Ops, SparseCore 0:
  45.3 111.8 all-reduce.3
  159.9 93.6 all-gather.2
where the time goes:
time: 279 us; the launch traced here: 278 us
  waiting for transfers between devices  163 us (58%)
  blocking collectives  44.4 us (16%)
  local copies, waits for them, and re-layouts  31.8 us (11%)
  between operations  15.5 us (6%)
  matrix products  14.4 us (5%)
  other arithmetic  6.04 us (2%)
    all_gather x1, waiting for transfers between devices, shards(): lax.all_gather(resid0, 'dp', axis=0, tiled=True)  94.8 us
    psum x1, waiting for transfers between devices, shards(): summed_grad = lax.psum(local_grad, 'dp')  64.2 us
    pmax x1, blocking collectives, shards(): step_size = 1.0 / lax.pmax(local_max, 'dp')  44.4 us
    unnamed x39, local copies, waits for them, and re-layouts  15.1 us
    while x60, local copies, waits for them, and re-layouts  7.65 us
  transfers between devices with their start and end apart: 4, of which 4 were waited for; matrix products, arithmetic and copies ran while one was open for 1% of the time, Pallas kernels for 0%

commit v1 on v0

--- a/solution.py
+++ b/solution.py
@@ -117,7 +117,7 @@
     )
     last_sent, stored_grads, stored_slopes = lax.fori_loop(0, tick_count, one_tick, start_state)
     local_grad = back_weight(inputs[0], stored_slopes[0])
-    summed_grad = lax.psum(local_grad, "dp")
+    summed_grad = jnp.sum(lax.all_gather(local_grad, "dp"), axis=0)
     mean_grad = summed_grad / lax.axis_size("dp")
     a_rows = a_factor[0]
     row_total = a_rows.shape[0]

time: 279 us -> 264 us (0.946)
  waiting for transfers between devices: 163 us -> 144 us
  other arithmetic: 6.04 us -> 11.6 us
    all_gather x0 -> x1, waiting for transfers between devices: none -> 87.7 us  [shards(): summed_grad = jnp.sum(lax.all_gather(local_grad, 'dp'), axis=0)]
    psum x1 -> x0, waiting for transfers between devices: 64.2 us -> none  [shards(): summed_grad = lax.psum(local_grad, 'dp')]
    all_gather x1, waiting for transfers between devices: 94.8 us -> 52.6 us  [shards(): lax.all_gather(resid0, 'dp', axis=0, tiled=True)]
    reduce_sum x0 -> x1, other arithmetic: none -> 3.48 us  [shards(): summed_grad = jnp.sum(lax.all_gather(local_grad, 'dp'), axis=0)]
  transfers between devices with their start and end apart: 4 -> 4, of which waited for: 4 -> 4; matrix products, arithmetic and copies ran while one was open for 1% -> 17% of each run, Pallas kernels for 0% -> 0%
where the time goes in v1:
time: 264 us; the launch traced here: 263 us
  waiting for transfers between devices  144 us (55%)
  blocking collectives  44.1 us (17%)
  local copies, waits for them, and re-layouts  31 us (12%)
  between operations  15.5 us (6%)
  matrix products  13.7 us (5%)
  other arithmetic  11.6 us (4%)
  starting transfers between devices  2.64 us (1%)
    all_gather x1, waiting for transfers between devices, shards(): summed_grad = jnp.sum(lax.all_gather(local_grad, 'dp'), axis=0)  87.7 us
    all_gather x1, waiting for transfers between devices, shards(): lax.all_gather(resid0, 'dp', axis=0, tiled=True)  52.6 us
    pmax x1, blocking collectives, shards(): step_size = 1.0 / lax.pmax(local_max, 'dp')  44.1 us
    unnamed x39, local copies, waits for them, and re-layouts  15.2 us
    while x60, local copies, waits for them, and re-layouts  7.65 us
    dot_general x2, matrix products, shards(): jnp.dot(left_cols, lax.all_gather(resid0, 'dp', axis=0, tiled=True), pref...  5.34 us
  transfers between devices with their start and end apart: 4, of which 4 were waited for; matrix products, arithmetic and copies ran while one was open for 17% of the time, Pallas kernels for 0%

profile of v1, /device:TPU:0, one launch (start us, length us, event | category | flops | bytes accessed | tf_op | source)
XLA Modules:
  0.0 263.1 jit_solution(1806504358141330044)
XLA Ops:
  7.2 1.3 fusion.56
  9.1 44.1 %pmax.7 = f32[]{:T(128)} all-reduce(f32[]{:T(128)} %reduce_max.18), channel_id=1, replica_groups=mesh['section'=2,'dp'=16] {'dp'}, use_global_device_ids=true, to_apply=%region_4.5 | all-reduce | flops 1 | bytes 8 | tf_op jit(solution)/shard_map/pmax | solution.py:127
  53.9 1.9 fusion.128
  56.4 0.9 copy.18
  60.7 2.3 reshape.70
  64.4 24.1 %while.20 = (s32[]{:T(128)}, bf16[64,2,2,128]{3,2,1,0:T(2,128)(2,1)}, bf16[1,64,2,2,128]{4,3,2,1,0:T(2,128)(2,1)}, bf16[1,64,2,2,128]{4,3,2,1,0:T(2,128)(2,1)}, ...) while((s32[]{:T(128)}, ...), condition=%wide.region_1.2_spmd.clone, body=%wide.region_0.1_spmd.clone.sunk | while | flops 113475592 | bytes 10772739 | solution.py:118
  64.4 1.3 collective-permute-start
  65.7 2.0 collective-permute-done
  67.7 1.7 fusion.172
  73.5 1.5 fusion.199
  76.4 1.3 collective-permute-start
  77.7 2.0 collective-permute-done
  79.7 1.7 fusion.172
  85.5 1.5 fusion.199
  88.4 0.9 reshape_squeeze.7
  89.3 2.9 %convolution_bitcast_fusion = f32[1,1728,64]{1,2,0:T(8,128)} fusion(bf16[1728,512]{1,0:T(8,128)(2,1)} %reshape.70, bf16[64,512]{1,0:T(8,128)(2,1)S(1)} %reshape_squeeze.7), kind=kOutput, calls=%fused_computation.116 | convolution fusion | flops 113246208 | bytes 2277376 | tf_op jit(solution)/shard_map/dot_general | solution.py:58
  93.9 52.6 %all-gather.6.cloned.1.call-done = bf16[16,108,1728]{2,1,0:T(8,128)(2,1)} async-done(((bf16[1,108,1728]{2,1,0:T(8,128)(2,1)}), bf16[16,108,1728]{2,1,0:T(8,128)(2,1)}) %all-gather.6.cloned.1.call-update) | async-done | bytes 5971984 | tf_op jit(solution)/shard_map/all_gather | solution.py:133
  146.5 8.8 %reshape.73 = bf16[1728,1728]{1,0:T(8,128)(2,1)} reshape(bf16[16,108,1728]{2,1,0:T(8,128)(2,1)} %all-gather.6.cloned.1.call-done) | data formatting | bytes 11943936
  155.3 4.3 %convolution_convert_fusion.1 = bf16[108,1728]{1,0:T(8,128)(2,1)S(1)} fusion(bf16[1728,1728]{1,0:T(8,128)(2,1)} %reshape.73, bf16[1,108,1728]{2,1,0:T(8,128)(2,1)S(1)} %copy-done.2, f32[]{:T(128)S(6)} %div.12, s32[108]{0:T(128)S(1)} %iota_add_fusion), kind=kOutput, calls=%fused_computation.115 | convolution fusion | flops 646278912 | bytes 6718900 | tf_op jit(solution)/shard_map/dot_general | solution.py:131
  160.2 1.1 fusion.54
  161.2 1.7 copy.17
  162.9 87.7 %all-gather.8.cloned.1.call-done = f32[16,1728,64]{1,2,0:T(8,128)} async-done(((f32[1,1728,64]{1,2,0:T(8,128)}), f32[16,1728,64]{1,2,0:T(8,128)}) %all-gather.8.cloned.1.call-update) | async-done | bytes 7077904 | tf_op jit(solution)/shard_map/all_gather | solution.py:120
  250.6 3.5 %reduce_sum.28 = f32[1728,64]{0,1:T(8,128)S(1)} reduce(f32[16,1728,64]{1,2,0:T(8,128)} %all-gather.8.cloned.1.call-done, f32[]{:T(128)} %constant.76.clone.1), dimensions={0}, to_apply=%region_5.6 | reduce | flops 1658880 | bytes 7520260 | tf_op jit(solution)/shard_map/reduce_sum | solution.py:120
  254.7 1.6 convolution_bitcast_fusion.1
  (122 shorter events, 18.9 us)
Async XLA Ops:
  7.2 48.8 %copy-start.5 = (bf16[1,64,1728]{2,1,0:T(8,128)(2,1)S(1)}, bf16[1,64,1728]{2,1,0:T(8,128)(2,1)}, u32[]{:S(2)}) copy-start(bf16[1,64,1728]{2,1,0:T(8,128)(2,1)} %param.11) | copy-start | bytes 663556
  7.2 50.2 %copy-start.1 = (bf16[1,1,1,64,2,2,128]{6,5,4,3,2,1,0:T(2,128)(2,1)S(1)}, bf16[1,1,1,64,2,2,128]{6,5,4,3,2,1,0:T(2,128)(2,1)}, u32[]{:S(2)}) copy-start(bf16[1,1,1,64,2,2,128]{6,5,4,3,2,1,0:T(2,128)(2,1)} %param.8) | copy-start | bytes 196612
  7.2 139.3 %all-gather.6.cloned.1.call-start = ((), (), s32[]{:S(2)}) async-start(), calls=%async_computation | async-start | bytes 6823936 | tf_op jit(solution)/shard_map/all_gather | solution.py:133
  55.9 194.7 %all-gather.8.cloned.1.call-start = ((), (), s32[]{:S(2)}) async-start(), calls=%async_computation.1 | async-start | bytes 7798784 | tf_op jit(solution)/shard_map/all_gather | solution.py:120
  64.4 3.3 %collective-permute-start = (bf16[64,2,2,128]{3,2,1,0:T(2,128)(2,1)}, bf16[64,2,2,128]{3,2,1,0:T(2,128)(2,1)S(1)}, u32[]{:S(2)}, u32[]{:S(2)}) collective-permute-start(bf16[64,2,2,128]{3,2,1,0:T(2,128)(2,1)} %get-tuple-element.362), channel_id=1, source_target_pairs={{16,0},{17,1},{18,2},{19,3},{20,4},{21,5},{22,6},{23,7},{24,8},{25... | collective-permute-start | bytes 196616 | tf_op jit(solution)/shard_map/while/body/eval_jaxpr/ppermute | solution.py:13
  73.5 2.2 copy-start.3
  75.8 0.6 copy-start.4
  76.4 3.3 %collective-permute-start = (bf16[64,2,2,128]{3,2,1,0:T(2,128)(2,1)}, bf16[64,2,2,128]{3,2,1,0:T(2,128)(2,1)S(1)}, u32[]{:S(2)}, u32[]{:S(2)}) collective-permute-start(bf16[64,2,2,128]{3,2,1,0:T(2,128)(2,1)} %get-tuple-element.362), channel_id=1, source_target_pairs={{16,0},{17,1},{18,2},{19,3},{20,4},{21,5},{22,6},{23,7},{24,8},{25... | collective-permute-start | bytes 196616 | tf_op jit(solution)/shard_map/while/body/eval_jaxpr/ppermute | solution.py:13
  85.5 2.2 copy-start.3
  87.8 0.6 copy-start.4
  88.4 3.8 %copy-start.6 = (bf16[1,64,64]{2,1,0:T(8,128)(2,1)S(1)}, bf16[1,64,64]{2,1,0:T(8,128)(2,1)}, u32[]{:S(2)}) copy-start(bf16[1,64,64]{2,1,0:T(8,128)(2,1)} %param.13) | copy-start | bytes 24580
  93.9 61.3 %copy-start.2 = (bf16[1,108,1728]{2,1,0:T(8,128)(2,1)S(1)}, bf16[1,108,1728]{2,1,0:T(8,128)(2,1)}, u32[]{:S(2)}) copy-start(bf16[1,108,1728]{2,1,0:T(8,128)(2,1)} %param.12) | copy-start | bytes 1119748
  155.3 4.9 %copy-start = (bf16[1728,1728]{1,0:T(8,128)(2,1)S(1)}, bf16[1728,1728]{1,0:T(8,128)(2,1)}, u32[]{:S(2)}) copy-start(bf16[1728,1728]{1,0:T(8,128)(2,1)} %reshape.73) | copy-start | bytes 17915908
Sparse Core Ops, SparseCore 0:
  56.0 90.4 all-gather.5
  149.2 101.3 all-gather.7
